TPU v7x, 512 devices: a whole 4x8x8 slice. The times are simulated.
512 devices in a mesh: section: 8 (over z), kv: 64 (over x, y, core).
Axes of the slice: x: 4, y: 8, z: 8, core: 2. Of those that a mesh axis runs over, the one named last changes fastest.
Arguments:
- held: bfloat16 [8, 128, 8192], P('section', None, 'kv'), may hold values from -6 to 6
- fresh: bfloat16 [1, 128, 8192], P(None, None, 'kv'), may hold values from -6 to 6
- block_starts: int32 [8], replicated, may hold values from 12288 to 24576
- fresh_starts: int32 [1], replicated, may hold values from 12288 to 24576
- norm_gain: float32 [8, 8192], P('section'), may hold values from 0.25 to 1.75
- w_qkv: bfloat16 [8, 8192, 5120], P('section', None, 'kv'), may hold values from -0.0625 to 0.0625
- w_out: bfloat16 [8, 4096, 8192], P('section', None, 'kv'), may hold values from -12 to 12
- cache_keys: bfloat16 [8, 24576, 512], P('section', 'kv'), may hold values from -400 to 400
- cache_values: bfloat16 [8, 24576, 512], P('section', 'kv'), may hold values from -6 to 6
- cache_lengths: int32 [8, 64], P('section', 'kv'), may hold values from 96 to 384, as said below
Outputs:
- produced: bfloat16 [8, 2, 128, 8192], P('section', None, None, 'kv')
Inputs may be any that keep to these rules, and one draw needn't show every extreme that they name: `cache_lengths`: each section has one block filled to 384.
All inputs are finite; a program needn't handle non-finite values.
Results may differ from a plain program's by a relative error of at most 0.017.
The roundings to bfloat16 on the way count: a program that leaves them out, or rounds other values in their place, can miss the bound.
Values may be sent and summed in bfloat16 or wider, within the bound.
No kernel may reach another device: no remote copies, remote signals or barrier semaphores. Data moves between devices by JAX's collectives and lax.ppermute only.
A program may use at most 128 MiB of HBM per device.

v0:
```python
import jax
import jax.numpy as jnp
from jax import lax
from jax.sharding import PartitionSpec as P

HD = 128
HEADS_Q = 32
KV_HEADS = 4


def passed_along(block, axis, distance):
    devices = range(lax.axis_size(axis))
    route = [(i - distance, i) for i in devices if i - distance in devices]
    return lax.ppermute(block, axis, route)


def block_partial(query, key_rows, value_rows, valid):
    row_count = query.shape[0]
    head_count = query.shape[1]
    head_width = query.shape[2]
    group_count = key_rows.shape[1]
    group_size = head_count // group_count
    shaped = jnp.transpose(
        query.reshape(row_count, group_count, group_size, head_width), (1, 0, 2, 3)
    )
    key_major = jnp.transpose(key_rows, (1, 0, 2))
    value_major = jnp.transpose(value_rows, (1, 0, 2))
    allowed = valid[:, None, :]

    def one_group(packed):
        group_query, group_keys, group_values = packed
        scores = jnp.einsum(
            "tgd,id->tgi", group_query, group_keys, preferred_element_type=jnp.float32
        ) * head_width ** (-0.5)
        row_max = jnp.max(jnp.where(allowed, scores, -1e30), axis=2)
        expo = jnp.where(allowed, jnp.exp(scores - row_max[..., None]), 0.0)
        row_sum = jnp.sum(expo, axis=2)
        weights = expo.astype(jnp.bfloat16)
        weighted = jnp.einsum(
            "tgi,id->tgd", weights, group_values, preferred_element_type=jnp.float32
        )
        return (row_max, row_sum, weighted)

    maxima, totals, sums = lax.map(one_group, (shaped, key_major, value_major))
    maxima = jnp.transpose(maxima, (1, 0, 2)).reshape(row_count, head_count)
    totals = jnp.transpose(totals, (1, 0, 2)).reshape(row_count, head_count)
    sums = jnp.transpose(sums, (1, 0, 2, 3)).reshape(row_count, head_count * head_width)
    return (maxima, totals, sums)


def combine_two(left_part, right_part):
    head_count = left_part[0].shape[1]
    row_count = left_part[0].shape[0]
    overall = jnp.maximum(left_part[0], right_part[0])
    left_factor = jnp.exp(left_part[0] - overall)
    right_factor = jnp.exp(right_part[0] - overall)
    total = left_part[1] * left_factor + right_part[1] * right_factor
    left_sum = left_part[2].reshape(row_count, head_count, -1) * left_factor[..., None]
    right_sum = right_part[2].reshape(row_count, head_count, -1) * right_factor[..., None]
    return (overall, total, (left_sum + right_sum).reshape(row_count, -1))


def merge_stack(maxima, totals, sums):
    count = maxima.shape[0]
    row_count = maxima.shape[1]
    head_count = maxima.shape[2]
    overall = jnp.max(maxima, axis=0)
    factor = jnp.exp(maxima - overall)
    total = jnp.sum(totals * factor, axis=0)
    summed = jnp.sum(sums.reshape(count, row_count, head_count, -1) * factor[..., None], axis=0)
    return (summed / total[..., None]).reshape(row_count, -1).astype(jnp.bfloat16)


def on_device(
    held,
    fresh,
    block_starts,
    fresh_starts,
    norm_gain,
    w_qkv,
    w_out,
    cache_keys,
    cache_values,
    cache_lengths,
):
    kv_index = lax.axis_index("kv")
    section_index = lax.axis_index("section")
    tick_count = fresh.shape[0] + 1
    row_count = held.shape[1]
    slot_count = cache_keys.shape[1]
    key_rows = cache_keys[0].reshape(slot_count, KV_HEADS, HD)
    value_rows = cache_values[0].reshape(slot_count, KV_HEADS, HD)
    filled = cache_lengths[0, 0]
    gain = norm_gain[0]
    weight_in = w_qkv[0]
    weight_out = w_out[0]
    slot_ids = jnp.arange(slot_count, dtype=jnp.int32)
    positions = kv_index * slot_count + slot_ids
    row_ids = jnp.arange(row_count, dtype=jnp.int32)
    causal = row_ids[None, :] <= row_ids[:, None]
    current = held[0]
    results = []
    for tick_index in range(tick_count):
        if tick_index > 0:
            passed = passed_along(current, "section", 1)
            current = jnp.where(section_index == 0, fresh[tick_index - 1], passed)
        anchor = section_index - tick_index
        start = jnp.where(
            anchor >= 0,
            block_starts[jnp.maximum(anchor, 0)],
            fresh_starts[jnp.clip(-anchor - 1, 0, tick_count - 2)],
        )
        gathered = lax.all_gather(current, "kv", axis=1, tiled=True)
        wide = gathered.astype(jnp.float32)
        normed = (
            wide * lax.rsqrt(jnp.mean(wide * wide, axis=1, keepdims=True) + 1e-05) * gain
        ).astype(jnp.bfloat16)
        local_cols = jnp.dot(normed, weight_in, preferred_element_type=jnp.float32).astype(
            jnp.bfloat16
        )
        united = lax.all_gather(local_cols, "kv", axis=1, tiled=True)
        query = united[:, : HEADS_Q * HD].reshape(row_count, HEADS_Q, HD)
        new_keys = united[:, HEADS_Q * HD : (HEADS_Q + KV_HEADS) * HD].reshape(
            row_count, KV_HEADS, HD
        )
        new_values = united[:, (HEADS_Q + KV_HEADS) * HD :].reshape(row_count, KV_HEADS, HD)
        usable = (slot_ids < filled) & (positions < start)
        valid = jnp.broadcast_to(usable[None, :], (row_count, slot_count))
        partial_value = block_partial(query, key_rows, value_rows, valid)

        def with_own(parts):
            return combine_two(parts, block_partial(query, new_keys, new_values, causal))

        def without_own(parts):
            return parts

        partial_value = lax.cond(kv_index == 0, with_own, without_own, partial_value)
        received = (
            lax.all_to_all(partial_value[0][None], "kv", split_axis=1, concat_axis=0, tiled=True),
            lax.all_to_all(partial_value[1][None], "kv", split_axis=1, concat_axis=0, tiled=True),
            lax.all_to_all(partial_value[2][None], "kv", split_axis=1, concat_axis=0, tiled=True),
        )
        attended = merge_stack(received[0], received[1], received[2])
        branch = jnp.dot(
            lax.all_gather(attended, "kv", axis=0, tiled=True),
            weight_out,
            preferred_element_type=jnp.float32,
        )
        current = (current.astype(jnp.float32) + branch).astype(jnp.bfloat16)
        results.append(current)
    return jnp.stack(results, 0)[None]


def solution(mesh):
    in_specs = (
        P("section", None, "kv"),
        P(None, None, "kv"),
        P(),
        P(),
        P("section", None),
        P("section", None, "kv"),
        P("section", None, "kv"),
        P("section", "kv", None),
        P("section", "kv", None),
        P("section", "kv"),
    )
    out_specs = P("section", None, None, "kv")
    return jax.shard_map(
        on_device, mesh=mesh, in_specs=in_specs, out_specs=out_specs, check_vma=False
    )
```

profile of v0, /device:TPU:1, one launch (start us, length us, event | category | flops | bytes accessed | tf_op | source)
XLA Modules:
  0.0 792.7 jit_solution(17048475888363732458)
XLA Ops:
  7.3 86.4 %all-gather.16.cloned.1.call-done = bf16[1,128,8192]{2,1,0:T(8,128)(2,1)} async-done(((bf16[1,128,128]{2,1,0:T(8,128)(2,1)}), bf16[1,128,8192]{2,1,0:T(8,128)(2,1)}) %all-gather.16.cloned.1.call-update) | async-done | bytes 2097168 | tf_op jit(solution)/shard_map/all_gather | solution.py:113
  93.7 2.2 fusion.77
  96.0 1.6 fusion.97
  103.6 75.6 %all-gather.10.cloned.1.call-done = bf16[128,5120]{0,1:T(8,128)(2,1)} async-done(((bf16[128,80]{0,1:T(8,128)(2,1)}), bf16[128,5120]{0,1:T(8,128)(2,1)}) %all-gather.10.cloned.1.call-update) | async-done | bytes 1310736 | tf_op jit(solution)/shard_map/all_gather | solution.py:121
  182.1 13.5 %while.58 = (s32[]{:T(128)}, f32[4,128,8]{1,2,0:T(8,128)S(1)}, f32[4,128,8]{1,2,0:T(8,128)S(1)}, f32[4,128,8,128]{3,1,2,0:T(8,128)S(1)}, bf16[4,128,8,128]{3,1,2...) while((s32[]{:T(128)}, f32[4,128,8]{1,2,0:T(8,128)S(1)}, ...), condition=%wide.region_4.5_spmd.clone, body=%wide.region_1.4_spmd.clone.sunk | while | flops 204863488 | bytes 5737833 | solution.py:44
  182.1 1.5 select_reduce_fusion.8
  184.1 1.3 fusion.142
  185.5 1.5 select_reduce_fusion.8
  187.5 1.3 fusion.142
  188.9 1.5 select_reduce_fusion.8
  190.9 1.3 fusion.142
  192.2 1.5 select_reduce_fusion.8
  195.6 12.1 %conditional.2 = (f32[128,32]{0,1:T(8,128)S(1)}, f32[128,32]{0,1:T(8,128)S(1)}, f32[128,4096]{1,0:T(8,128)}) conditional(s32[]{:T(128)} %convert_element_type.53, (f32[128,4,8,128]{3,0,2,1:T(8,128)S(1)}, f32[128,32]{0,1:T(8,128)S(1)}, f32[128,32]{0,1:T(8,128)S(1)}) %tuple.192, (bf16[128,4096]{0,1:T(8,128)(2,1)}, bf16[128,5120]{0,1:T(8,128)(2,1)}, ...), branch_computations={%region_5.6_spmd, %region_6.11_spmd} | conditional | flops 69883904 | bytes 51759524 | solution.py:137
  196.8 3.0 copy.131
  208.4 25.7 %all-to-all-start.2 = ((f32[1,128,32]{2,0,1:T(1,128)}), f32[1,128,32]{2,0,1:T(1,128)S(1)}, u32[]{:S(2)}, u32[]{:S(2)}) async-start(f32[1,128,32]{2,0,1:T(1,128)} %bitcast.73), calls=%async_computation.2 | async-start | bytes 131072 | tf_op jit(solution)/shard_map/all_to_all | solution.py:140
  234.8 9.2 %all-to-all-done.2 = f32[1,128,32]{2,0,1:T(1,128)S(1)} async-done(((f32[1,128,32]{2,0,1:T(1,128)}), f32[1,128,32]{2,0,1:T(1,128)S(1)}, u32[]{:S(2)}, u32[]{:S(2)}) %all-to-all-start.2) | async-done | bytes 16416 | tf_op jit(solution)/shard_map/all_to_all | solution.py:140
  244.0 4.4 all-to-all-start.1
  248.4 5.3 broadcast_in_dim.169
  253.8 4.5 all-to-all-done.1
  258.3 5.9 all-to-all-start
  265.9 49.5 %all-to-all-done = f32[1,128,4096]{2,0,1:T(1,128)S(1)} async-done(((f32[1,128,4096]{2,0,1:T(1,128)}), f32[1,128,4096]{2,0,1:T(1,128)S(1)}, u32[]{:S(2)}, u32[]{:S(2)}) %all-to-all-start) | async-done | bytes 2097184 | tf_op jit(solution)/shard_map/all_to_all | solution.py:141
  316.0 4.3 multiply_reduce_fusion.1
  321.1 79.2 %all-gather.18.cloned.1.call-done = bf16[64,2,4096]{2,1,0:T(2,128)(2,1)} async-done(((bf16[1,2,4096]{2,1,0:T(2,128)(2,1)}), bf16[64,2,4096]{2,1,0:T(2,128)(2,1)}) %all-gather.18.cloned.1.call-update) | async-done | bytes 1048592 | tf_op jit(solution)/shard_map/all_gather | solution.py:145
  400.3 1.5 reshape.190
  402.2 3.3 collective-permute-start
  407.3 78.1 %all-gather.12.cloned.1.call-done = bf16[128,8192]{1,0:T(8,128)(2,1)} async-done(((bf16[128,128]{1,0:T(8,128)(2,1)}), bf16[128,8192]{1,0:T(8,128)(2,1)}) %all-gather.12.cloned.1.call-update) | async-done | bytes 2097168 | tf_op jit(solution)/shard_map/all_gather | solution.py:113
  485.5 2.2 fusion.74
  487.7 1.6 fusion.92
  489.4 81.6 %all-gather.14.cloned.1.call-done = bf16[128,5120]{0,1:T(8,128)(2,1)} async-done(((bf16[128,80]{0,1:T(8,128)(2,1)}), bf16[128,5120]{0,1:T(8,128)(2,1)}) %all-gather.14.cloned.1.call-update) | async-done | bytes 1310736 | tf_op jit(solution)/shard_map/all_gather | solution.py:121
  573.9 13.5 %while.59 = (s32[]{:T(128)}, f32[4,128,8]{1,2,0:T(8,128)S(1)}, f32[4,128,8]{1,2,0:T(8,128)S(1)}, f32[4,128,8,128]{3,1,2,0:T(8,128)S(1)}, bf16[4,128,8,128]{3,1,2...) while((s32[]{:T(128)}, f32[4,128,8]{1,2,0:T(8,128)S(1)}, ...), condition=%wide.region_18.19_spmd.clone, body=%wide.region_15.18_spmd.clone.sunk | while | flops 204863488 | bytes 5737833 | solution.py:44
  573.9 1.5 select_reduce_fusion.9
  577.3 1.5 select_reduce_fusion.9
  579.3 1.3 fusion.146
  580.6 1.5 select_reduce_fusion.9
  584.0 1.5 select_reduce_fusion.9
  586.0 1.3 fusion.146
  587.4 4.4 conditional.3
  588.6 3.0 copy.132
  592.5 24.2 %all-to-all-start.5 = ((f32[1,128,32]{2,0,1:T(1,128)}), f32[1,128,32]{2,0,1:T(1,128)S(1)}, u32[]{:S(2)}, u32[]{:S(2)}) async-start(f32[1,128,32]{2,0,1:T(1,128)} %bitcast.95), calls=%async_computation.5 | async-start | bytes 131072 | tf_op jit(solution)/shard_map/all_to_all | solution.py:140
  617.4 9.2 %all-to-all-done.5 = f32[1,128,32]{2,0,1:T(1,128)S(1)} async-done(((f32[1,128,32]{2,0,1:T(1,128)}), f32[1,128,32]{2,0,1:T(1,128)S(1)}, u32[]{:S(2)}, u32[]{:S(2)}) %all-to-all-start.5) | async-done | bytes 16416 | tf_op jit(solution)/shard_map/all_to_all | solution.py:140
  626.6 4.4 all-to-all-start.4
  631.0 5.3 broadcast_in_dim.172
  636.3 4.5 all-to-all-done.4
  640.9 5.9 all-to-all-start.3
  647.1 50.9 %all-to-all-done.3 = f32[1,128,4096]{2,0,1:T(1,128)S(1)} async-done(((f32[1,128,4096]{2,0,1:T(1,128)}), f32[1,128,4096]{2,0,1:T(1,128)S(1)}, u32[]{:S(2)}, u32[]{:S(2)}) %all-to-all-start.3) | async-done | bytes 2097184 | tf_op jit(solution)/shard_map/all_to_all | solution.py:141
  698.6 4.3 multiply_reduce_fusion
  703.6 79.3 %all-gather.20.cloned.1.call-done = bf16[64,2,4096]{2,1,0:T(2,128)(2,1)} async-done(((bf16[1,2,4096]{2,1,0:T(2,128)(2,1)}), bf16[64,2,4096]{2,1,0:T(2,128)(2,1)}) %all-gather.20.cloned.1.call-update) | async-done | bytes 1048592 | tf_op jit(solution)/shard_map/all_gather | solution.py:145
  782.9 1.5 reshape.192
  (109 shorter events, 31.6 us)
Async XLA Ops:
  6.5 89.4 %copy-start = (bf16[1,8192,80]{1,2,0:T(8,128)(2,1)S(1)}, bf16[1,8192,80]{1,2,0:T(8,128)(2,1)}, u32[]{:S(2)}) copy-start(bf16[1,8192,80]{1,2,0:T(8,128)(2,1)} %param.27) | copy-start | bytes 3932164
  6.5 89.4 %copy-start.27 = (f32[1,8192]{1,0:T(1,128)S(1)}, f32[1,8192]{1,0:T(1,128)}, u32[]{:S(2)}) copy-start(f32[1,8192]{1,0:T(1,128)} %param.26) | copy-start | bytes 98308
  6.5 87.1 %all-gather.16.cloned.1.call-start = ((), (), s32[]{:S(2)}) async-start(), calls=%async_computation.9 | async-start | bytes 2129920 | tf_op jit(solution)/shard_map/all_gather | solution.py:113
  7.3 172.0 %all-gather.10.cloned.1.call-start = ((), (), s32[]{:S(2)}) async-start(), calls=%async_computation.6 | async-start | bytes 1331200 | tf_op jit(solution)/shard_map/all_gather | solution.py:121
  93.7 2.3 copy-start.9
  95.9 1.7 copy-start.13
  95.9 2.9 copy-start.14
  97.6 3.7 copy-start.26
  180.5 1.3 copy-start.2
  208.4 35.6 %all-to-all-start.2 = ((f32[1,128,32]{2,0,1:T(1,128)}), f32[1,128,32]{2,0,1:T(1,128)S(1)}, u32[]{:S(2)}, u32[]{:S(2)}) async-start(f32[1,128,32]{2,0,1:T(1,128)} %bitcast.73), calls=%async_computation.2 | async-start | bytes 131072 | tf_op jit(solution)/shard_map/all_to_all | solution.py:140
  244.0 9.8 %copy-start.16 = (f32[1,128,32]{2,0,1:T(1,128)}, f32[1,128,32]{2,0,1:T(1,128)S(1)}, u32[]{:S(2)}) copy-start(f32[1,128,32]{2,0,1:T(1,128)S(1)} %all-to-all-done.2) | copy-start | bytes 49156
  244.0 14.3 %all-to-all-start.1 = ((f32[1,128,32]{2,0,1:T(1,128)}), f32[1,128,32]{2,0,1:T(1,128)S(1)}, u32[]{:S(2)}, u32[]{:S(2)}) async-start(f32[1,128,32]{2,0,1:T(1,128)} %bitcast.70), calls=%async_computation.1 | async-start | bytes 131072 | tf_op jit(solution)/shard_map/all_to_all | solution.py:139
  258.3 57.1 %all-to-all-start = ((f32[1,128,4096]{2,0,1:T(1,128)}), f32[1,128,4096]{2,0,1:T(1,128)S(1)}, u32[]{:S(2)}, u32[]{:S(2)}) async-start(f32[1,128,4096]{2,0,1:T(1,128)} %broadcast_in_dim.169), calls=%async_computation | async-start | bytes 4194304 | tf_op jit(solution)/shard_map/all_to_all | solution.py:141
  264.2 136.0 %all-gather.18.cloned.1.call-start = ((), (), s32[]{:S(2)}) async-start(), calls=%async_computation.10 | async-start | bytes 1064960 | tf_op jit(solution)/shard_map/all_gather | solution.py:145
  320.3 81.4 %copy-start.7 = (bf16[1,4096,128]{2,1,0:T(8,128)(2,1)S(1)}, bf16[1,4096,128]{2,1,0:T(8,128)(2,1)}, u32[]{:S(2)}) copy-start(bf16[1,4096,128]{2,1,0:T(8,128)(2,1)} %param.28) | copy-start | bytes 3145732
  320.3 81.4 %copy-start.21 = (bf16[1,128,128]{2,1,0:T(8,128)(2,1)S(1)}, bf16[1,128,128]{2,1,0:T(8,128)(2,1)}, u32[]{:S(2)}) copy-start(bf16[1,128,128]{2,1,0:T(8,128)(2,1)} %param.22) | copy-start | bytes 98308
  321.0 85.5 %copy-start.25 = (bf16[1,128,128]{2,1,0:T(8,128)(2,1)S(1)}, bf16[1,128,128]{2,1,0:T(8,128)(2,1)}, u32[]{:S(2)}) copy-start(bf16[1,128,128]{2,1,0:T(8,128)(2,1)} %param.23) | copy-start | bytes 98308
  321.0 164.5 %all-gather.12.cloned.1.call-start = ((), (), s32[]{:S(2)}) async-start(), calls=%async_computation.7 | async-start | bytes 2129920 | tf_op jit(solution)/shard_map/all_gather | solution.py:113
  401.7 86.0 %copy-start.28 = (f32[1,8192]{1,0:T(1,128)S(1)}, f32[1,8192]{1,0:T(1,128)}, u32[]{:S(2)}) copy-start(f32[1,8192]{1,0:T(1,128)} %param.26) | copy-start | bytes 98308
  402.2 87.2 %copy-start.22 = (bf16[128,128]{1,0:T(8,128)(2,1)}, bf16[128,128]{1,0:T(8,128)(2,1)S(1)}, u32[]{:S(2)}) copy-start(bf16[128,128]{1,0:T(8,128)(2,1)S(1)} %fusion.91) | copy-start | bytes 98308
  402.2 4.3 collective-permute-start
  407.1 163.9 %all-gather.14.cloned.1.call-start = ((), (), s32[]{:S(2)}) async-start(), calls=%async_computation.8 | async-start | bytes 1331200 | tf_op jit(solution)/shard_map/all_gather | solution.py:121
  485.5 2.3 copy-start.10
  572.3 1.6 copy-start.24
  592.5 34.1 %all-to-all-start.5 = ((f32[1,128,32]{2,0,1:T(1,128)}), f32[1,128,32]{2,0,1:T(1,128)S(1)}, u32[]{:S(2)}, u32[]{:S(2)}) async-start(f32[1,128,32]{2,0,1:T(1,128)} %bitcast.95), calls=%async_computation.5 | async-start | bytes 131072 | tf_op jit(solution)/shard_map/all_to_all | solution.py:140
  626.6 14.3 %all-to-all-start.4 = ((f32[1,128,32]{2,0,1:T(1,128)}), f32[1,128,32]{2,0,1:T(1,128)S(1)}, u32[]{:S(2)}, u32[]{:S(2)}) async-start(f32[1,128,32]{2,0,1:T(1,128)} %bitcast.92), calls=%async_computation.4 | async-start | bytes 131072 | tf_op jit(solution)/shard_map/all_to_all | solution.py:139
  640.9 57.1 %all-to-all-start.3 = ((f32[1,128,4096]{2,0,1:T(1,128)}), f32[1,128,4096]{2,0,1:T(1,128)S(1)}, u32[]{:S(2)}, u32[]{:S(2)}) async-start(f32[1,128,4096]{2,0,1:T(1,128)} %broadcast_in_dim.172), calls=%async_computation.3 | async-start | bytes 4194304 | tf_op jit(solution)/shard_map/all_to_all | solution.py:141
  646.8 136.1 %all-gather.20.cloned.1.call-start = ((), (), s32[]{:S(2)}) async-start(), calls=%async_computation.11 | async-start | bytes 1064960 | tf_op jit(solution)/shard_map/all_gather | solution.py:145
  702.9 81.5 %copy-start.8 = (bf16[1,4096,128]{2,1,0:T(8,128)(2,1)S(1)}, bf16[1,4096,128]{2,1,0:T(8,128)(2,1)}, u32[]{:S(2)}) copy-start(bf16[1,4096,128]{2,1,0:T(8,128)(2,1)} %param.28) | copy-start | bytes 3145732
  702.9 81.5 %copy-start.15 = (bf16[128,128]{1,0:T(8,128)(2,1)S(1)}, bf16[128,128]{1,0:T(8,128)(2,1)}, u32[]{:S(2)}) copy-start(bf16[128,128]{1,0:T(8,128)(2,1)} %bitcast_select_fusion) | copy-start | bytes 98308
  703.6 81.2 %copy-start.23 = (bf16[128,128]{1,0:T(8,128)(2,1)S(1)}, bf16[128,128]{1,0:T(8,128)(2,1)}, u32[]{:S(2)}) copy-start(bf16[128,128]{1,0:T(8,128)(2,1)} %copy-done.22) | copy-start | bytes 98308
  703.6 81.8 %copy-start.1 = (bf16[1,8192,80]{1,2,0:T(8,128)(2,1)S(1)}, bf16[1,8192,80]{1,2,0:T(8,128)(2,1)}, u32[]{:S(2)}) copy-start(bf16[1,8192,80]{1,2,0:T(8,128)(2,1)} %param.27) | copy-start | bytes 3932164
Sparse Core Ops, SparseCore 0:
  10.5 83.1 all-gather.15
  97.7 81.4 all-gather.9
  321.1 79.0 all-gather.17
  407.2 78.1 all-gather.11
  489.5 81.4 all-gather.13
  703.7 79.1 all-gather.19
where the time goes:
time: 800 us; the launch traced here: 793 us
  waiting for transfers between devices  610 us (76%)
  starting transfers between devices  74.2 us (9%)
  local copies, waits for them, and re-layouts  35 us (4%)
  matrix products  26.5 us (3%)
  other arithmetic  22.1 us (3%)
  between operations  16.8 us (2%)
  loops' own time  8.38 us (1%)
    all_gather x2, waiting for transfers between devices, on_device(): gathered = lax.all_gather(current, 'kv', axis=1, tiled=True)  164 us
    all_gather x2, waiting for transfers between devices, on_device(): lax.all_gather(attended, 'kv', axis=0, tiled=True)  158 us
    all_gather x2, waiting for transfers between devices, on_device(): united = lax.all_gather(local_cols, 'kv', axis=1, tiled=True)  157 us
    all_to_all x2, waiting for transfers between devices, on_device(): lax.all_to_all(partial_value[2][None], 'kv', split_axis=1, concat_axis=0,...  100 us
    all_to_all x2, starting transfers between devices, on_device(): lax.all_to_all(partial_value[1][None], 'kv', split_axis=1, concat_axis=0,...  49.9 us
    all_to_all x2, waiting for transfers between devices, on_device(): lax.all_to_all(partial_value[1][None], 'kv', split_axis=1, concat_axis=0,...  18.3 us
  transfers between devices with their start and end apart: 13, of which 13 were waited for; matrix products, arithmetic and copies ran while one was open for 2% of the time, Pallas kernels for 0%

commit v1 on v0

--- a/solution.py
+++ b/solution.py
@@ -118,7 +118,15 @@
         local_cols = jnp.dot(normed, weight_in, preferred_element_type=jnp.float32).astype(
             jnp.bfloat16
         )
-        united = lax.all_gather(local_cols, "kv", axis=1, tiled=True)
+        united = jnp.concatenate(
+            lax.all_to_all(
+                jnp.stack([local_cols] * lax.axis_size("kv"), 0),
+                axis_name="kv",
+                split_axis=0,
+                concat_axis=0,
+            ),
+            1,
+        )
         query = united[:, : HEADS_Q * HD].reshape(row_count, HEADS_Q, HD)
         new_keys = united[:, HEADS_Q * HD : (HEADS_Q + KV_HEADS) * HD].reshape(
             row_count, KV_HEADS, HD

time: 800 us -> 717 us (0.90)
  waiting for transfers between devices: 610 us -> 480 us
  blocking collectives: 0 us -> 42.2 us
    all_gather x2 -> x0, waiting for transfers between devices: 157 us -> none  [on_device(): united = lax.all_gather(local_cols, 'kv', axis=1, tiled=True)]
    all_to_all x0 -> x1, blocking collectives: none -> 42.2 us  [on_device(): lax.all_to_all(jnp.stack([local_cols] * lax.axis_size('kv'), 0), axis_nam...]
    all_to_all x0 -> x1, waiting for transfers between devices: none -> 26.9 us  [on_device(): lax.all_to_all(jnp.stack([local_cols] * lax.axis_size('kv'), 0), axis_nam...]
    all_to_all x0 -> x1, starting transfers between devices: none -> 8.07 us  [on_device(): lax.all_to_all(jnp.stack([local_cols] * lax.axis_size('kv'), 0), axis_nam...]
  transfers between devices with their start and end apart: 13 -> 12, of which waited for: 13 -> 12; matrix products, arithmetic and copies ran while one was open for 2% -> 3% of each run, Pallas kernels for 0% -> 0%
where the time goes in v1:
time: 717 us; the launch traced here: 709 us
  waiting for transfers between devices  480 us (67%)
  starting transfers between devices  79.9 us (11%)
  blocking collectives  42.2 us (6%)
  local copies, waits for them, and re-layouts  34.4 us (5%)
  matrix products  25.2 us (4%)
  other arithmetic  22.1 us (3%)
  between operations  16.5 us (2%)
  loops' own time  9.29 us (1%)
    all_gather x2, waiting for transfers between devices, on_device(): gathered = lax.all_gather(current, 'kv', axis=1, tiled=True)  165 us
    all_gather x2, waiting for transfers between devices, on_device(): lax.all_gather(attended, 'kv', axis=0, tiled=True)  158 us
    all_to_all x2, waiting for transfers between devices, on_device(): lax.all_to_all(partial_value[2][None], 'kv', split_axis=1, concat_axis=0,...  100 us
    all_to_all x2, starting transfers between devices, on_device(): lax.all_to_all(partial_value[1][None], 'kv', split_axis=1, concat_axis=0,...  47.9 us
    all_to_all x1, blocking collectives, on_device(): lax.all_to_all(jnp.stack([local_cols] * lax.axis_size('kv'), 0), axis_nam...  42.2 us
    all_to_all x1, waiting for transfers between devices, on_device(): lax.all_to_all(jnp.stack([local_cols] * lax.axis_size('kv'), 0), axis_nam...  26.9 us
    all_to_all x2, waiting for transfers between devices, on_device(): lax.all_to_all(partial_value[1][None], 'kv', split_axis=1, concat_axis=0,...  18.3 us
  transfers between devices with their start and end apart: 12, of which 12 were waited for; matrix products, arithmetic and copies ran while one was open for 3% of the time, Pallas kernels for 0%

profile of v1, /device:TPU:1, one launch (start us, length us, event | category | flops | bytes accessed | tf_op | source)
XLA Modules:
  0.0 709.4 jit_solution(13345825434212861684)
XLA Ops:
  7.3 86.4 %all-gather.10.cloned.1.call-done = bf16[1,128,8192]{2,1,0:T(8,128)(2,1)} async-done(((bf16[1,128,128]{2,1,0:T(8,128)(2,1)}), bf16[1,128,8192]{2,1,0:T(8,128)(2,1)}) %all-gather.10.cloned.1.call-update) | async-done | bytes 2097168 | tf_op jit(solution)/shard_map/all_gather | solution.py:113
  93.7 2.2 fusion.77
  98.2 8.1 %all-to-all-start = ((bf16[64,128,80]{1,2,0:T(8,128)(2,1)}), bf16[64,128,80]{1,2,0:T(8,128)(2,1)S(1)}, u32[]{:S(2)}, u32[]{:S(2)}) async-start(bf16[64,128,80]{1,2,0:T(8,128)(2,1)} %stack.10), calls=%async_computation | async-start | bytes 2621440 | tf_op jit(solution)/shard_map/all_to_all | solution.py:122
  113.5 26.9 %all-to-all-done = bf16[64,128,80]{1,2,0:T(8,128)(2,1)S(1)} async-done(((bf16[64,128,80]{1,2,0:T(8,128)(2,1)}), bf16[64,128,80]{1,2,0:T(8,128)(2,1)S(1)}, u32[]{:S(2)}, u32[]{:S(2)}) %all-to-all-start) | async-done | bytes 1310752 | tf_op jit(solution)/shard_map/all_to_all | solution.py:122
  142.1 13.6 %while.58 = (s32[]{:T(128)}, f32[4,128,8]{1,2,0:T(8,128)S(1)}, f32[4,128,8]{1,2,0:T(8,128)S(1)}, f32[4,128,8,128]{3,1,2,0:T(8,128)S(1)}, bf16[4,128,8,128]{1,3,2...) while((s32[]{:T(128)}, f32[4,128,8]{1,2,0:T(8,128)S(1)}, ...), condition=%wide.region_4.5_spmd.clone, body=%wide.region_1.4_spmd.clone.sunk | while | flops 204863488 | bytes 5737833 | solution.py:44
  142.1 1.5 select_reduce_fusion.8
  144.1 1.3 fusion.142
  145.5 1.5 select_reduce_fusion.8
  147.5 1.3 fusion.142
  148.9 1.5 select_reduce_fusion.8
  150.9 1.3 fusion.142
  152.3 1.5 select_reduce_fusion.8
  154.3 1.3 fusion.142
  155.7 13.0 %conditional.2 = (f32[128,32]{0,1:T(8,128)S(1)}, f32[128,32]{0,1:T(8,128)S(1)}, f32[128,4096]{1,0:T(8,128)}) conditional(s32[]{:T(128)} %convert_element_type.53, (f32[128,4,8,128]{3,0,2,1:T(8,128)S(1)}, f32[128,32]{0,1:T(8,128)S(1)}, f32[128,32]{0,1:T(8,128)S(1)}) %tuple.191, (bf16[128,4096]{0,1:T(8,128)(2,1)}, bf16[128,5120]{0,1:T(8,128)(2,1)}, ...), branch_computations={%region_5.6_spmd, %region_6.11_spmd} | conditional | flops 69883904 | bytes 51759524 | solution.py:145
  156.9 3.0 copy.129
  169.4 24.3 %all-to-all-start.3 = ((f32[1,128,32]{2,0,1:T(1,128)}), f32[1,128,32]{2,0,1:T(1,128)S(1)}, u32[]{:S(2)}, u32[]{:S(2)}) async-start(f32[1,128,32]{2,0,1:T(1,128)} %bitcast.76), calls=%async_computation.3 | async-start | bytes 131072 | tf_op jit(solution)/shard_map/all_to_all | solution.py:148
  194.4 9.2 %all-to-all-done.3 = f32[1,128,32]{2,0,1:T(1,128)S(1)} async-done(((f32[1,128,32]{2,0,1:T(1,128)}), f32[1,128,32]{2,0,1:T(1,128)S(1)}, u32[]{:S(2)}, u32[]{:S(2)}) %all-to-all-start.3) | async-done | bytes 16416 | tf_op jit(solution)/shard_map/all_to_all | solution.py:148
  203.5 4.4 all-to-all-start.2
  207.9 5.3 broadcast_in_dim.169
  213.2 4.6 all-to-all-done.2
  217.8 5.9 all-to-all-start.1
  225.4 49.5 %all-to-all-done.1 = f32[1,128,4096]{2,0,1:T(1,128)S(1)} async-done(((f32[1,128,4096]{2,0,1:T(1,128)}), f32[1,128,4096]{2,0,1:T(1,128)S(1)}, u32[]{:S(2)}, u32[]{:S(2)}) %all-to-all-start.1) | async-done | bytes 2097184 | tf_op jit(solution)/shard_map/all_to_all | solution.py:149
  275.5 4.3 multiply_reduce_fusion.1
  280.5 79.2 %all-gather.12.cloned.1.call-done = bf16[64,2,4096]{2,1,0:T(2,128)(2,1)} async-done(((bf16[1,2,4096]{2,1,0:T(2,128)(2,1)}), bf16[64,2,4096]{2,1,0:T(2,128)(2,1)}) %all-gather.12.cloned.1.call-update) | async-done | bytes 1048592 | tf_op jit(solution)/shard_map/all_gather | solution.py:153
  359.7 1.5 reshape.210
  361.7 3.3 collective-permute-start
  366.6 78.3 %all-gather.8.cloned.1.call-done = bf16[128,8192]{1,0:T(8,128)(2,1)} async-done(((bf16[128,128]{1,0:T(8,128)(2,1)}), bf16[128,8192]{1,0:T(8,128)(2,1)}) %all-gather.8.cloned.1.call-update) | async-done | bytes 2097168 | tf_op jit(solution)/shard_map/all_gather | solution.py:113
  445.0 2.2 fusion.74
  448.4 42.2 %all_to_all.82 = bf16[64,128,80]{1,2,0:T(8,128)(2,1)S(1)} all-to-all(bf16[64,128,80]{1,2,0:T(8,128)(2,1)S(1)} %stack.12), channel_id=1, replica_groups=mesh['section'=8,'kv'=64] {'kv'}, dimensions={0} | all-to-all | bytes 2621440 | tf_op jit(solution)/shard_map/all_to_all | solution.py:122
  491.7 13.3 %while.59 = (s32[]{:T(128)}, f32[4,128,8]{1,2,0:T(8,128)S(1)}, f32[4,128,8]{1,2,0:T(8,128)S(1)}, f32[4,128,8,128]{3,1,2,0:T(8,128)S(1)}, bf16[4,128,8,128]{1,3,2...) while((s32[]{:T(128)}, f32[4,128,8]{1,2,0:T(8,128)S(1)}, ...), condition=%wide.region_18.19_spmd.clone, body=%wide.region_15.18_spmd.clone.sunk | while | flops 204863488 | bytes 5737961 | solution.py:44
  491.7 1.4 select_reduce_fusion.9
  493.7 1.3 fusion.146
  495.1 1.4 select_reduce_fusion.9
  497.0 1.3 fusion.146
  498.4 1.4 select_reduce_fusion.9
  501.7 1.4 select_reduce_fusion.9
  505.0 4.4 conditional.3
  506.2 3.0 copy.130
  510.1 23.7 %all-to-all-start.7 = ((f32[1,128,32]{2,0,1:T(1,128)}), f32[1,128,32]{2,0,1:T(1,128)S(1)}, u32[]{:S(2)}, u32[]{:S(2)}) async-start(f32[1,128,32]{2,0,1:T(1,128)} %bitcast.101), calls=%async_computation.7 | async-start | bytes 131072 | tf_op jit(solution)/shard_map/all_to_all | solution.py:148
  534.5 9.2 %all-to-all-done.7 = f32[1,128,32]{2,0,1:T(1,128)S(1)} async-done(((f32[1,128,32]{2,0,1:T(1,128)}), f32[1,128,32]{2,0,1:T(1,128)S(1)}, u32[]{:S(2)}, u32[]{:S(2)}) %all-to-all-start.7) | async-done | bytes 16416 | tf_op jit(solution)/shard_map/all_to_all | solution.py:148
  543.7 4.4 all-to-all-start.6
  548.1 5.3 broadcast_in_dim.172
  553.4 4.6 all-to-all-done.6
  558.0 5.9 all-to-all-start.5
  564.1 50.9 %all-to-all-done.5 = f32[1,128,4096]{2,0,1:T(1,128)S(1)} async-done(((f32[1,128,4096]{2,0,1:T(1,128)}), f32[1,128,4096]{2,0,1:T(1,128)S(1)}, u32[]{:S(2)}, u32[]{:S(2)}) %all-to-all-start.5) | async-done | bytes 2097184 | tf_op jit(solution)/shard_map/all_to_all | solution.py:149
  615.6 4.3 multiply_reduce_fusion
  620.6 79.3 %all-gather.14.cloned.1.call-done = bf16[64,2,4096]{2,1,0:T(2,128)(2,1)} async-done(((bf16[1,2,4096]{2,1,0:T(2,128)(2,1)}), bf16[64,2,4096]{2,1,0:T(2,128)(2,1)}) %all-gather.14.cloned.1.call-update) | async-done | bytes 1048592 | tf_op jit(solution)/shard_map/all_gather | solution.py:153
  699.9 1.5 reshape.212
  (106 shorter events, 31.5 us)
Async XLA Ops:
  6.5 89.4 %copy-start = (bf16[1,8192,80]{1,2,0:T(8,128)(2,1)S(1)}, bf16[1,8192,80]{1,2,0:T(8,128)(2,1)}, u32[]{:S(2)}) copy-start(bf16[1,8192,80]{1,2,0:T(8,128)(2,1)} %param.27) | copy-start | bytes 3932164
  6.5 89.4 %copy-start.27 = (f32[1,8192]{1,0:T(1,128)S(1)}, f32[1,8192]{1,0:T(1,128)}, u32[]{:S(2)}) copy-start(f32[1,8192]{1,0:T(1,128)} %param.26) | copy-start | bytes 98308
  6.5 87.1 %all-gather.10.cloned.1.call-start = ((), (), s32[]{:S(2)}) async-start(), calls=%async_computation.9 | async-start | bytes 2129920 | tf_op jit(solution)/shard_map/all_gather | solution.py:113
  93.7 2.3 copy-start.10
  97.0 9.4 %copy-start.14 = (bf16[1,384,512]{2,1,0:T(8,128)(2,1)S(1)}, bf16[1,384,512]{2,1,0:T(8,128)(2,1)}, u32[]{:S(2)}) copy-start(bf16[1,384,512]{2,1,0:T(8,128)(2,1)} %param.29) | copy-start | bytes 1179652
  98.2 42.2 %all-to-all-start = ((bf16[64,128,80]{1,2,0:T(8,128)(2,1)}), bf16[64,128,80]{1,2,0:T(8,128)(2,1)S(1)}, u32[]{:S(2)}, u32[]{:S(2)}) async-start(bf16[64,128,80]{1,2,0:T(8,128)(2,1)} %stack.10), calls=%async_computation | async-start | bytes 2621440 | tf_op jit(solution)/shard_map/all_to_all | solution.py:122
  106.3 4.6 copy-start.26
  140.4 1.4 copy-start.6
  169.4 34.2 %all-to-all-start.3 = ((f32[1,128,32]{2,0,1:T(1,128)}), f32[1,128,32]{2,0,1:T(1,128)S(1)}, u32[]{:S(2)}, u32[]{:S(2)}) async-start(f32[1,128,32]{2,0,1:T(1,128)} %bitcast.76), calls=%async_computation.3 | async-start | bytes 131072 | tf_op jit(solution)/shard_map/all_to_all | solution.py:148
  203.5 9.7 %copy-start.16 = (f32[1,128,32]{2,0,1:T(1,128)}, f32[1,128,32]{2,0,1:T(1,128)S(1)}, u32[]{:S(2)}) copy-start(f32[1,128,32]{2,0,1:T(1,128)S(1)} %all-to-all-done.3) | copy-start | bytes 49156
  203.5 14.3 %all-to-all-start.2 = ((f32[1,128,32]{2,0,1:T(1,128)}), f32[1,128,32]{2,0,1:T(1,128)S(1)}, u32[]{:S(2)}, u32[]{:S(2)}) async-start(f32[1,128,32]{2,0,1:T(1,128)} %bitcast.73), calls=%async_computation.2 | async-start | bytes 131072 | tf_op jit(solution)/shard_map/all_to_all | solution.py:147
  217.8 57.1 %all-to-all-start.1 = ((f32[1,128,4096]{2,0,1:T(1,128)}), f32[1,128,4096]{2,0,1:T(1,128)S(1)}, u32[]{:S(2)}, u32[]{:S(2)}) async-start(f32[1,128,4096]{2,0,1:T(1,128)} %broadcast_in_dim.169), calls=%async_computation.1 | async-start | bytes 4194304 | tf_op jit(solution)/shard_map/all_to_all | solution.py:149
  223.7 136.1 %all-gather.12.cloned.1.call-start = ((), (), s32[]{:S(2)}) async-start(), calls=%async_computation.10 | async-start | bytes 1064960 | tf_op jit(solution)/shard_map/all_gather | solution.py:153
  279.8 81.4 %copy-start.8 = (bf16[1,4096,128]{2,1,0:T(8,128)(2,1)S(1)}, bf16[1,4096,128]{2,1,0:T(8,128)(2,1)}, u32[]{:S(2)}) copy-start(bf16[1,4096,128]{2,1,0:T(8,128)(2,1)} %param.28) | copy-start | bytes 3145732
  279.8 81.4 %copy-start.21 = (bf16[1,128,128]{2,1,0:T(8,128)(2,1)S(1)}, bf16[1,128,128]{2,1,0:T(8,128)(2,1)}, u32[]{:S(2)}) copy-start(bf16[1,128,128]{2,1,0:T(8,128)(2,1)} %param.22) | copy-start | bytes 98308
  280.5 85.5 %copy-start.25 = (bf16[1,128,128]{2,1,0:T(8,128)(2,1)S(1)}, bf16[1,128,128]{2,1,0:T(8,128)(2,1)}, u32[]{:S(2)}) copy-start(bf16[1,128,128]{2,1,0:T(8,128)(2,1)} %param.23) | copy-start | bytes 98308
  280.5 164.5 %all-gather.8.cloned.1.call-start = ((), (), s32[]{:S(2)}) async-start(), calls=%async_computation.8 | async-start | bytes 2129920 | tf_op jit(solution)/shard_map/all_gather | solution.py:113
  361.2 86.0 %copy-start.28 = (f32[1,8192]{1,0:T(1,128)S(1)}, f32[1,8192]{1,0:T(1,128)}, u32[]{:S(2)}) copy-start(f32[1,8192]{1,0:T(1,128)} %param.26) | copy-start | bytes 98308
  361.7 86.6 %copy-start.22 = (bf16[128,128]{1,0:T(8,128)(2,1)}, bf16[128,128]{1,0:T(8,128)(2,1)S(1)}, u32[]{:S(2)}) copy-start(bf16[128,128]{1,0:T(8,128)(2,1)S(1)} %fusion.91) | copy-start | bytes 98308
  361.7 4.3 collective-permute-start
  445.0 2.3 copy-start.11
  490.6 1.1 copy-start.7
  490.6 1.1 copy-start.24
  510.1 33.6 %all-to-all-start.7 = ((f32[1,128,32]{2,0,1:T(1,128)}), f32[1,128,32]{2,0,1:T(1,128)S(1)}, u32[]{:S(2)}, u32[]{:S(2)}) async-start(f32[1,128,32]{2,0,1:T(1,128)} %bitcast.101), calls=%async_computation.7 | async-start | bytes 131072 | tf_op jit(solution)/shard_map/all_to_all | solution.py:148
  543.7 14.3 %all-to-all-start.6 = ((f32[1,128,32]{2,0,1:T(1,128)}), f32[1,128,32]{2,0,1:T(1,128)S(1)}, u32[]{:S(2)}, u32[]{:S(2)}) async-start(f32[1,128,32]{2,0,1:T(1,128)} %bitcast.98), calls=%async_computation.6 | async-start | bytes 131072 | tf_op jit(solution)/shard_map/all_to_all | solution.py:147
  558.0 57.1 %all-to-all-start.5 = ((f32[1,128,4096]{2,0,1:T(1,128)}), f32[1,128,4096]{2,0,1:T(1,128)S(1)}, u32[]{:S(2)}, u32[]{:S(2)}) async-start(f32[1,128,4096]{2,0,1:T(1,128)} %broadcast_in_dim.172), calls=%async_computation.5 | async-start | bytes 4194304 | tf_op jit(solution)/shard_map/all_to_all | solution.py:149
  563.8 136.1 %all-gather.14.cloned.1.call-start = ((), (), s32[]{:S(2)}) async-start(), calls=%async_computation.11 | async-start | bytes 1064960 | tf_op jit(solution)/shard_map/all_gather | solution.py:153
  619.9 81.4 %copy-start.9 = (bf16[1,4096,128]{2,1,0:T(8,128)(2,1)S(1)}, bf16[1,4096,128]{2,1,0:T(8,128)(2,1)}, u32[]{:S(2)}) copy-start(bf16[1,4096,128]{2,1,0:T(8,128)(2,1)} %param.28) | copy-start | bytes 3145732
  619.9 81.4 %copy-start.15 = (bf16[128,128]{1,0:T(8,128)(2,1)S(1)}, bf16[128,128]{1,0:T(8,128)(2,1)}, u32[]{:S(2)}) copy-start(bf16[128,128]{1,0:T(8,128)(2,1)} %bitcast_select_fusion) | copy-start | bytes 98308
  620.6 81.2 %copy-start.23 = (bf16[128,128]{1,0:T(8,128)(2,1)S(1)}, bf16[128,128]{1,0:T(8,128)(2,1)}, u32[]{:S(2)}) copy-start(bf16[128,128]{1,0:T(8,128)(2,1)} %copy-done.22) | copy-start | bytes 98308
  620.6 81.8 %copy-start.1 = (bf16[1,8192,80]{1,2,0:T(8,128)(2,1)S(1)}, bf16[1,8192,80]{1,2,0:T(8,128)(2,1)}, u32[]{:S(2)}) copy-start(bf16[1,8192,80]{1,2,0:T(8,128)(2,1)} %param.27) | copy-start | bytes 3932164
Sparse Core Ops, SparseCore 0:
  10.5 83.1 all-gather.9
  280.6 79.1 all-gather.11
  366.7 78.1 all-gather.7
  620.7 79.1 all-gather.13
